TPU v7x, 128 devices: a whole 4x4x4 slice. The times are simulated.
128 devices in a mesh: dp: 8 (over z, core), ctx: 16 (over y, x).
Axes of the slice: x: 4, y: 4, z: 4, core: 2. Of those that a mesh axis runs over, the one named last changes fastest.
Arguments:
- ids: int32 [8, 4096, 8], P('dp', 'ctx'), may hold values from 0 to 1023
- tables: bfloat16 [8, 1024, 1024], P(None, 'dp', 'ctx'), may hold values from -2.09375 to 2.09375
- w_qkv: bfloat16 [1024, 3072], P('dp'), may hold values from -5 to 5
- w_out: bfloat16 [1024, 1024], P('dp'), may hold values from -0.1875 to 0.1875
- attn_gain: float32 [1024], replicated, may hold values from 0.1 to 1.9
- conv_gain: float32 [1024], replicated, may hold values from 0.1 to 1.9
- conv_kernel: float32 [31, 1024], replicated, may hold values from -1 to 1
- back_list: int32 [16, 2], replicated, may hold values from 0 to 17, as said below
- ahead_list: int32 [16, 1], replicated, may hold values from 1 to 17, as said below
- cotangent: bfloat16 [8, 4096, 1024], P('dp', 'ctx'), may hold values from -8 to 8
Outputs:
- block_out: bfloat16 [8, 4096, 1024], P('dp', 'ctx')
- grad_embedded: bfloat16 [8, 4096, 1024], P('dp', 'ctx')
- grad_qkv: float32 [1024, 3072], P('dp')
- grad_out: float32 [1024, 1024], P('dp')
- grad_kernel: float32 [31, 1024], replicated
Inputs may be any that keep to these rules, and one draw needn't show every extreme that they name: `back_list`: row b lists distinct blocks among b - 2 .. b - 1 that exist, first, then the filler 16 + 1; block 2 and the last block list all 2, the first none. `ahead_list`: row b lists distinct blocks among b + 1 .. b + 1 that exist, first, then the filler 16 + 1; block 0 lists all 1, the last none.
All inputs are finite; a program needn't handle non-finite values.
Results may differ from a plain program's by a relative error of at most 0.015.
Values may be sent and summed in bfloat16 or wider, within the bound.
No kernel may reach another device: no remote copies, remote signals or barrier semaphores. Data moves between devices by JAX's collectives and lax.ppermute only.
A program may use at most 128 MiB of HBM per device.

v0:
```python
import jax
import jax.numpy as jnp
from jax import lax
from jax.sharding import PartitionSpec as P

HEADS = 16
EPSILON = 1e-06
NEGATIVE = -1e30


def from_behind(value, axis, steps):
    count = lax.axis_size(axis)
    first, last = (max(0, -steps), min(count, count - steps))
    return lax.ppermute(value, axis, [(source, source + steps) for source in range(first, last)])


def with_halo(block, sides, width):
    for axis, dim in sides:
        count = lax.axis_size(axis)
        forward = [(i, i + 1) for i in range(count - 1)]
        backward = [(target, source) for source, target in forward]
        low = lax.ppermute(
            lax.slice_in_dim(block, block.shape[dim] - width, None, axis=dim), axis, forward
        )
        high = lax.ppermute(lax.slice_in_dim(block, 0, width, axis=dim), axis, backward)
        block = jnp.concatenate([low, block, high], axis=dim)
    return block


def inverse_rms(features):
    return lax.rsqrt(jnp.mean(features * features, axis=-1, keepdims=True) + EPSILON)


def norm_back(features, inverse, gains, upstream):
    inner = jnp.mean(features * gains * upstream, axis=-1, keepdims=True)
    return inverse * gains * upstream - features * inverse * inverse * inverse * inner


def silu_slope(conv_sum):
    sigmoid = jax.nn.sigmoid(conv_sum)
    return sigmoid * (1.0 + conv_sum * (1.0 - sigmoid))


def block_scores(queries, key_block, listed_block, score_scale):
    return jnp.where(
        listed_block,
        jnp.einsum("rqhd,rkhd->rhqk", queries, key_block, preferred_element_type=jnp.float32)
        * score_scale,
        NEGATIVE,
    )


def probabilities(queries, key_part, listed, score_scale):
    pieces = [
        block_scores(queries, key_part[:, position], listed[position], score_scale)
        for position in range(key_part.shape[1])
    ]
    scores = jnp.concatenate(pieces, axis=3)
    highest = jnp.max(scores, axis=3, keepdims=True)
    weights = jnp.exp(scores - highest)
    return weights / jnp.sum(weights, axis=3, keepdims=True)


def on_device(
    ids, tables, w_qkv, w_out, attn_gain, conv_gain, conv_kernel, back_list, ahead_list, cotangent
):
    recordings = ids.shape[0]
    frames_dev = ids.shape[1]
    head_count = HEADS
    tap_count = conv_kernel.shape[0]
    rim_width = (tap_count - 1) // 2
    group_width = 4
    group_count = head_count // group_width
    ids_whole = lax.all_gather(ids, "ctx", axis=1, tiled=True)
    table_whole = lax.all_gather(tables, "dp", axis=1, tiled=True)
    columns = jnp.zeros(ids_whole.shape[:2] + (table_whole.shape[2],), jnp.float32)
    for codebook in range(table_whole.shape[0]):
        columns = columns + jnp.take(
            table_whole[codebook], ids_whole[:, :, codebook], axis=0
        ).astype(jnp.float32)
    embedded = lax.all_to_all(
        columns.astype(jnp.bfloat16), "ctx", split_axis=1, concat_axis=2, tiled=True
    )
    weight_qkv, weight_out = (
        lax.all_gather(w_qkv, "dp", axis=0, tiled=True),
        lax.all_gather(w_out, "dp", axis=0, tiled=True),
    )
    model_width = weight_out.shape[0]
    head_size = model_width // head_count
    score_scale = head_size ** (-0.5)
    features = embedded.astype(jnp.float32).reshape(-1, model_width)
    attn_inverse = inverse_rms(features)
    normed = (features * attn_inverse * attn_gain).astype(jnp.bfloat16)
    projected = jnp.dot(normed, weight_qkv, preferred_element_type=jnp.float32).astype(jnp.bfloat16)
    projected = projected.reshape(recordings, frames_dev, 3 * model_width)
    own_pairs = projected[:, :, model_width:]
    ctx_index = lax.axis_index("ctx")
    back_row = lax.dynamic_index_in_dim(back_list, ctx_index, 0, keepdims=False)
    ahead_row = lax.dynamic_index_in_dim(ahead_list, ctx_index, 0, keepdims=False)
    offsets = [-(step + 1) for step in range(back_list.shape[1])] + [1]
    listed_items = [jnp.array(True)]
    pair_blocks = [own_pairs]
    for offset in offsets:
        list_row = back_row if offset < 0 else ahead_row
        listed_items.append(jnp.any(list_row == ctx_index + offset))
        pair_blocks.append(from_behind(own_pairs, "ctx", -offset))
    listed = jnp.stack(listed_items)
    seen_count = len(pair_blocks)
    stacked = jnp.stack(pair_blocks, axis=1)
    key_all = stacked[..., :model_width].reshape(
        recordings, seen_count, frames_dev, head_count, head_size
    )
    value_all = stacked[..., model_width:].reshape(
        recordings, seen_count, frames_dev, head_count, head_size
    )
    query_all = projected[:, :, :model_width].reshape(recordings, frames_dev, head_count, head_size)

    def forward_group(group):
        first_head = group * group_width
        queries = lax.dynamic_slice_in_dim(query_all, first_head, group_width, 2)
        key_part = lax.dynamic_slice_in_dim(key_all, first_head, group_width, 3)
        value_part = lax.dynamic_slice_in_dim(value_all, first_head, group_width, 3)
        probs_low = probabilities(queries, key_part, listed, score_scale).astype(jnp.bfloat16)
        value_flat = value_part.reshape(recordings, -1, group_width, head_size)
        return jnp.einsum(
            "rhqk,rkhd->rqhd", probs_low, value_flat, preferred_element_type=jnp.float32
        ).astype(jnp.bfloat16)

    mixed = lax.map(forward_group, jnp.arange(group_count, dtype=jnp.int32))
    mixed = jnp.moveaxis(mixed, 0, 2).reshape(recordings * frames_dev, model_width)
    projection = jnp.dot(mixed, weight_out, preferred_element_type=jnp.float32)
    middle = (features + projection).astype(jnp.bfloat16)
    middle_wide = middle.astype(jnp.float32)
    conv_inverse = inverse_rms(middle_wide)
    conv_input = (
        (middle_wide * conv_inverse * conv_gain)
        .astype(jnp.bfloat16)
        .reshape(recordings, frames_dev, model_width)
    )
    padded = with_halo(conv_input, (("ctx", 1),), rim_width).astype(jnp.float32)

    def conv_step(tap_index, sums):
        taps = lax.dynamic_index_in_dim(conv_kernel, tap_index, 0, keepdims=False)
        return sums + taps * lax.dynamic_slice_in_dim(padded, tap_index, frames_dev, 1)

    conv_sum = lax.fori_loop(
        0, tap_count, conv_step, jnp.zeros((recordings, frames_dev, model_width), jnp.float32)
    )
    middle_frames = middle_wide.reshape(recordings, frames_dev, model_width)
    block_out = (middle_frames + jax.nn.silu(conv_sum)).astype(jnp.bfloat16)
    upstream = cotangent.astype(jnp.float32)
    grad_conv_low = (upstream * silu_slope(conv_sum)).astype(jnp.bfloat16)
    grad_conv = lax.optimization_barrier(grad_conv_low).astype(jnp.float32)
    grad_padded = with_halo(grad_conv_low, (("ctx", 1),), rim_width).astype(jnp.float32)

    def back_step(tap_index, carry):
        grad_input, kernel_rows = carry
        window = lax.dynamic_slice_in_dim(padded, tap_index, frames_dev, 1)
        row = jnp.sum(grad_conv * window, axis=(0, 1))
        kernel_rows = lax.dynamic_update_index_in_dim(kernel_rows, row, tap_index, 0)
        taps = lax.dynamic_index_in_dim(conv_kernel, tap_index, 0, keepdims=False)
        start_row = 2 * rim_width - tap_index
        grad_input = grad_input + taps * lax.dynamic_slice_in_dim(
            grad_padded, start_row, frames_dev, 1
        )
        return (grad_input, kernel_rows)

    grad_input, kernel_rows = lax.fori_loop(
        0,
        tap_count,
        back_step,
        (
            jnp.zeros((recordings, frames_dev, model_width), jnp.float32),
            jnp.zeros((tap_count, model_width), jnp.float32),
        ),
    )
    grad_kernel = lax.psum(kernel_rows, ("dp", "ctx"))
    grad_middle = (
        upstream.reshape(-1, model_width)
        + norm_back(middle_wide, conv_inverse, conv_gain, grad_input.reshape(-1, model_width))
    ).astype(jnp.bfloat16)
    contract_rows = (((0,), (0,)), ((), ()))
    contract_columns = (((1,), (1,)), ((), ()))
    grad_mixed = lax.dot_general(
        grad_middle, weight_out, contract_columns, preferred_element_type=jnp.float32
    ).astype(jnp.bfloat16)
    grad_wout = lax.dot_general(
        mixed, grad_middle, contract_rows, preferred_element_type=jnp.float32
    )
    grad_heads = grad_mixed.reshape(recordings, frames_dev, head_count, head_size)

    def backward_group(group):
        first_head = group * group_width
        queries = lax.dynamic_slice_in_dim(query_all, first_head, group_width, 2)
        key_part = lax.dynamic_slice_in_dim(key_all, first_head, group_width, 3)
        value_part = lax.dynamic_slice_in_dim(value_all, first_head, group_width, 3)
        grad_part = lax.dynamic_slice_in_dim(grad_heads, first_head, group_width, 2)
        probs = probabilities(queries, key_part, listed, score_scale)
        probs_low = probs.astype(jnp.bfloat16)
        key_flat = key_part.reshape(recordings, -1, group_width, head_size)
        value_flat = value_part.reshape(recordings, -1, group_width, head_size)
        grad_probs = jnp.einsum(
            "rqhd,rkhd->rhqk", grad_part, value_flat, preferred_element_type=jnp.float32
        )
        row_sum = jnp.sum(probs * grad_probs, axis=3, keepdims=True)
        grad_scores = (probs * (grad_probs - row_sum) * score_scale).astype(jnp.bfloat16)
        grad_query = jnp.einsum(
            "rhqk,rkhd->rqhd", grad_scores, key_flat, preferred_element_type=jnp.float32
        )
        grad_key = jnp.einsum(
            "rhqk,rqhd->rkhd", grad_scores, queries, preferred_element_type=jnp.float32
        )
        grad_value = jnp.einsum(
            "rhqk,rqhd->rkhd", probs_low, grad_part, preferred_element_type=jnp.float32
        )
        return (grad_query, grad_key, grad_value)

    grad_query, grad_key, grad_value = lax.map(
        backward_group, jnp.arange(group_count, dtype=jnp.int32)
    )
    grad_query = jnp.moveaxis(grad_query, 0, 2).reshape(recordings * frames_dev, model_width)
    grad_key = jnp.moveaxis(grad_key, 0, 2).reshape(recordings, seen_count, frames_dev, model_width)
    grad_value = jnp.moveaxis(grad_value, 0, 2).reshape(
        recordings, seen_count, frames_dev, model_width
    )
    pair_total = jnp.concatenate([grad_key[:, 0], grad_value[:, 0]], axis=2)
    for position, offset in enumerate(offsets):
        outgoing = jnp.concatenate(
            [grad_key[:, position + 1], grad_value[:, position + 1]], axis=2
        ).astype(jnp.bfloat16)
        arrived = from_behind(outgoing, "ctx", offset)
        pair_total = pair_total + arrived.astype(jnp.float32)
    grad_projected = jnp.concatenate(
        [
            grad_query.astype(jnp.bfloat16),
            pair_total.reshape(recordings * frames_dev, 2 * model_width).astype(jnp.bfloat16),
        ],
        axis=1,
    )
    grad_wqkv = lax.dot_general(
        normed, grad_projected, contract_rows, preferred_element_type=jnp.float32
    )
    grad_normed = lax.dot_general(
        grad_projected, weight_qkv, contract_columns, preferred_element_type=jnp.float32
    )
    grad_embedded = (
        grad_middle.astype(jnp.float32) + norm_back(features, attn_inverse, attn_gain, grad_normed)
    ).astype(jnp.bfloat16)
    share_qkv, share_out = (
        lax.psum_scatter(grad_wqkv, ("dp", "ctx"), scatter_dimension=0, tiled=True),
        lax.psum_scatter(grad_wout, ("dp", "ctx"), scatter_dimension=0, tiled=True),
    )
    grad_qkv, grad_out = (
        lax.all_gather(share_qkv.astype(jnp.bfloat16), "ctx", axis=0, tiled=True).astype(
            share_qkv.dtype
        ),
        lax.all_gather(share_out.astype(jnp.bfloat16), "ctx", axis=0, tiled=True).astype(
            share_out.dtype
        ),
    )
    return (
        block_out,
        grad_embedded.reshape(recordings, frames_dev, model_width),
        grad_qkv,
        grad_out,
        grad_kernel,
    )


def solution(mesh):
    in_specs = (
        P("dp", "ctx", None),
        P(None, "dp", "ctx"),
        P("dp", None),
        P("dp", None),
        P(),
        P(),
        P(),
        P(),
        P(),
        P("dp", "ctx", None),
    )
    out_specs = (P("dp", "ctx", None), P("dp", "ctx", None), P("dp", None), P("dp", None), P())
    return jax.shard_map(
        on_device, mesh=mesh, in_specs=in_specs, out_specs=out_specs, check_vma=False
    )
```

profile of v0, /device:TPU:1, one launch (start us, length us, event | category | flops | bytes accessed | tf_op | source)
XLA Modules:
  0.0 1618.0 jit_solution(10427319216327694318)
XLA Ops:
  9.8 19.9 %all_gather.19 = s32[1,4096,8]{1,2,0:T(8,128)S(1)} all-gather(s32[1,256,8]{1,2,0:T(8,128)} %param.20), channel_id=1, replica_groups=mesh['dp'=8,'ctx'=16] {'ctx'}, dimensions={1}, use_global_device_ids=true | all-gather | bytes 139264 | tf_op jit(solution)/shard_map/all_gather | solution.py:74
  30.4 8.9 all-gather.4.cloned.1.call-done
  41.0 12.1 gather_fusion.2
  53.1 14.9 gather_fusion.3
  68.0 14.9 gather_fusion.4
  82.9 14.9 gather_fusion.5
  97.8 14.9 gather_fusion.6
  112.7 15.0 gather_fusion.7
  127.8 14.9 gather_fusion
  142.7 14.9 gather_fusion.1
  157.6 8.9 add_convert_fusion
  166.5 16.7 %copy.311 = bf16[1,4096,64]{2,0,1:T(2,128)(2,1)S(1)} copy(bf16[1,4096,64]{2,1,0:T(8,128)(2,1)S(1)} %add_convert_fusion) | data formatting | bytes 1048576 | tf_op jit(solution)/shard_map/convert_element_type | solution.py:82
  183.8 22.4 %reduce.51 = bf16[4096,64]{1,0:T(8,128)(2,1)S(1)} reduce(bf16[4096,1,64]{2,1,0:T(2,128)(2,1)S(1)} %bitcast.411, bf16[]{:T(256)} %broadcast.243), dimensions={1}, to_apply=%bitcast.323.reduce_sub_computation | reduce | bytes 1048578
  206.9 17.4 %all_to_all.4 = bf16[16,2,8192]{2,1,0:T(2,128)(2,1)S(1)} all-to-all(bf16[16,2,8192]{2,1,0:T(2,128)(2,1)S(1)} %reshape.824), channel_id=1, replica_groups=mesh['dp'=8,'ctx'=16] {'ctx'}, dimensions={0} | all-to-all | bytes 1048576 | tf_op jit(solution)/shard_map/all_to_all | solution.py:81
  247.7 11.2 collective-permute-done
  258.9 22.5 %collective-permute-done.1 = bf16[1,256,2048]{2,1,0:T(8,128)(2,1)} collective-permute-done((bf16[1,256,2048]{2,1,0:T(8,128)(2,1)S(1)}, bf16[1,256,2048]{2,1,0:T(8,128)(2,1)}, u32[]{:S(2)}, u32[]{:S(2)}) %collective-permute-start.1) | collective-permute-done | bytes 1048608 | tf_op jit(solution)/shard_map/ppermute | solution.py:14
  300.9 65.9 %while.56 = (s32[]{:T(128)}, bf16[4,1,256,4,64]{2,4,3,1,0:T(8,128)(2,1)}, s32[4]{0:T(128)S(1)}, bf16[1,4,256,16,64]{2,1,4,3,0:T(4,128)(2,1)}, bf16[1,256,16,64]{...) while((s32[]{:T(128)}, ...), condition=%wide.region_10.12_spmd, body=%wide.region_4.11_spmd.sunk | while | flops 282916864 | bytes 20639508 | solution.py:129
  379.7 40.1 %while.58 = (s32[]{:T(128)}, f32[1,256,1024]{2,1,0:T(8,128)S(1)}, f32[31,1024]{1,0:T(8,128)}, f32[1,286,1024]{2,1,0:T(8,128)S(1)}, s32[]{:T(128)}, /*index=5*/s32[]{:T(128)}) while((s32[]{:T(128)}, f32[1,256,1024]{2,1,0:T(8,128)S(1)}, f32[31,1024]{1,0:T(8,128)}, f32[1,286,1024]{2,1,0:T(8,128)S(1)}, s32[]{:T(128)}, ...), condition=%wide.region_13.15_spmd.clone, body=%wide.region_12.14_spmd.clone.sunk | while | flops 786435 | bytes 3158103 | solution.py:146
  431.7 130.4 %while.59 = (s32[]{:T(128)}, f32[1,256,1024]{2,1,0:T(8,128)S(1)}, f32[31,1024]{1,0:T(8,128)}, f32[31,1024]{1,0:T(8,128)}, f32[1,286,1024]{2,1,0:T(8,128)}, /*ind...) while((s32[]{:T(128)}, f32[1,256,1024]{2,1,0:T(8,128)S(1)}, ...), condition=%wide.region_16.18_spmd.clone, body=%wide.region_14.17_spmd.clone.sunk | while | flops 1309703 | bytes 5267637 | solution.py:168
  569.6 8.7 reduce-scatter.3.cloned.1.call-start
  578.3 157.8 %while.57 = (s32[]{:T(128)}, bf16[4,1,256,4,64]{2,4,3,1,0:T(8,128)(2,1)}, f32[4,1,1024,4,64]{2,4,3,1,0:T(8,128)}, f32[4,1,1024,4,64]{2,4,3,1,0:T(8,128)}, s32[4]...) while((s32[]{:T(128)}, ...), condition=%wide.region_25.27_spmd, body=%wide.region_18.26_spmd.sunk | while | flops 716965888 | bytes 64713528 | solution.py:218
  638.3 7.3 fusion.199
  717.2 7.3 fusion.199
  765.6 8.1 pad_maximum_fusion.1
  800.0 24.5 %collective-permute-done.8 = bf16[1,256,2048]{1,0,2:T(2,128)(2,1)S(1)} collective-permute-done((bf16[1,256,2048]{1,0,2:T(2,128)(2,1)}, bf16[1,256,2048]{1,0,2:T(2,128)(2,1)S(1)}, u32[]{:S(2)}, u32[]{:S(2)}) %collective-permute-start.8) | collective-permute-done | bytes 1048608 | tf_op jit(solution)/shard_map/ppermute | solution.py:14
  824.5 12.3 collective-permute-done.9
  836.8 19.2 %fusion.105 = bf16[1,256,2048]{1,0,2:T(2,128)(2,1)S(1)} fusion(bf16[1,256,2048]{1,0,2:T(2,128)(2,1)S(1)} %collective-permute-done.9, bf16[1,256,2048]{1,0,2:T(2,128)(2,1)S(1)} %collective-permute-done.8, f32[1,256,2048]{1,2,0:T(8,128)S(1)} %convert_element_type.227, f32[1,256,1024]{1,0,2:T(1,128)S(1)} %get-tuple-element.771, ...), kind=kLoop, calls=%fused_computation.122 | loop fusion | flops 3670016 | bytes 7340032 | tf_op jit(solution)/shard_map/convert_element_type | solution.py:236
  869.9 340.0 %reduce-scatter.5.cloned.1.call-done = f32[8,1024]{1,0:T(8,128)} async-done(((f32[1024,1024]{1,0:T(8,128)}), f32[8,1024]{1,0:T(8,128)}) %reduce-scatter.5.cloned.1.call-update) | async-done | bytes 32784 | tf_op jit(solution)/shard_map/reduce_scatter | solution.py:251
  1210.7 17.3 %all_gather.23 = bf16[128,1024]{1,0:T(8,128)(2,1)S(1)} all-gather(bf16[8,1024]{1,0:T(8,128)(2,1)S(1)} %convert_element_type.235), channel_id=1, replica_groups=mesh['dp'=8,'ctx'=16] {'ctx'}, dimensions={0}, use_global_device_ids=true | all-gather | bytes 278528 | tf_op jit(solution)/shard_map/all_gather | solution.py:257
  1228.8 235.0 %reduce-scatter.3.cloned.1.call-done = f32[8,3072]{1,0:T(8,128)} async-done(((f32[1024,3072]{1,0:T(8,128)}), f32[8,3072]{1,0:T(8,128)}) %reduce-scatter.3.cloned.1.call-update) | async-done | bytes 98320 | tf_op jit(solution)/shard_map/reduce_scatter | solution.py:250
  1464.6 16.9 %all_gather.22 = bf16[128,3072]{1,0:T(8,128)(2,1)S(1)} all-gather(bf16[8,3072]{1,0:T(8,128)(2,1)S(1)} %convert_element_type.233), channel_id=1, replica_groups=mesh['dp'=8,'ctx'=16] {'ctx'}, dimensions={0}, use_global_device_ids=true | all-gather | bytes 835584 | tf_op jit(solution)/shard_map/all_gather | solution.py:254
  1482.8 126.3 %all-reduce.2.cloned.1.call-done = f32[31,1024]{1,0:T(8,128)} async-done(((f32[31,1024]{1,0:T(8,128)}), f32[31,1024]{1,0:T(8,128)}) %all-reduce.2.cloned.1.call-update) | async-done | bytes 126992 | tf_op jit(solution)/shard_map/psum | solution.py:177
  (430 shorter events, 528.3 us)
Async XLA Ops:
  7.2 236.5 %copy-start = (s32[16,1]{0,1:T(1,128)S(1)}, s32[16,1]{0,1:T(1,128)}, u32[]{:S(2)}) copy-start(s32[16,1]{0,1:T(1,128)} %param.28) | copy-start | bytes 196
  7.2 32.2 %all-gather.4.cloned.1.call-start = ((), (), s32[]{:S(2)}) async-start(), calls=%async_computation.3 | async-start | bytes 2359296 | tf_op jit(solution)/shard_map/all_gather | solution.py:75
  9.0 220.5 %all-gather.6.cloned.1.call-start = ((), (), s32[]{:S(2)}) async-start(), calls=%async_computation.4 | async-start | bytes 7077888 | tf_op jit(solution)/shard_map/all_gather | solution.py:85
  9.8 357.1 %all-gather.8.cloned.1.call-start = ((), (), s32[]{:S(2)}) async-start(), calls=%async_computation.5 | async-start | bytes 2359296 | tf_op jit(solution)/shard_map/all_gather | solution.py:86
  142.7 14.9 copy-start.10
  229.2 5.6 copy-start.4
  229.5 15.4 copy-start.22
  236.0 23.0 %collective-permute-start = (bf16[1,256,2048]{2,1,0:T(8,128)(2,1)S(1)}, bf16[1,256,2048]{2,1,0:T(8,128)(2,1)}, u32[]{:S(2)}, u32[]{:S(2)}) collective-permute-start(bf16[1,256,2048]{2,1,0:T(8,128)(2,1)S(1)} %get-tuple-element.746), channel_id=1, source_target_pairs={{0,1},{1,2},{2,3},{3,4},{4,5},{5,6},{6,7},{7,8},{8,9},{9,10},{10,1... | collective-permute-start | bytes 3145736 | tf_op jit(solution)/shard_map/ppermute | solution.py:14
  239.1 42.3 %collective-permute-start.1 = (bf16[1,256,2048]{2,1,0:T(8,128)(2,1)S(1)}, bf16[1,256,2048]{2,1,0:T(8,128)(2,1)}, u32[]{:S(2)}, u32[]{:S(2)}) collective-permute-start(bf16[1,256,2048]{2,1,0:T(8,128)(2,1)S(1)} %get-tuple-element.746), channel_id=1, source_target_pairs={{0,2},{1,3},{2,4},{3,5},{4,6},{5,7},{6,8},{7,9},{8,10},{9,11},{10,... | collective-permute-start | bytes 3145736 | tf_op jit(solution)/shard_map/ppermute | solution.py:14
  242.2 44.1 %collective-permute-start.2 = (bf16[1,256,2048]{2,1,0:T(8,128)(2,1)S(1)}, bf16[1,256,2048]{2,1,0:T(8,128)(2,1)}, u32[]{:S(2)}, u32[]{:S(2)}) collective-permute-start(bf16[1,256,2048]{2,1,0:T(8,128)(2,1)S(1)} %get-tuple-element.746), channel_id=1, source_target_pairs={{1,0},{2,1},{3,2},{4,3},{5,4},{6,5},{7,6},{8,7},{9,8},{10,9},{11,1... | collective-permute-start | bytes 3145736 | tf_op jit(solution)/shard_map/ppermute | solution.py:14
  243.6 966.3 %reduce-scatter.5.cloned.1.call-start = ((), (), s32[]{:S(2)}) async-start(), calls=%async_computation.7 | async-start | bytes 4227072 | tf_op jit(solution)/shard_map/reduce_scatter | solution.py:251
  369.7 50.2 %copy-start.6 = (bf16[256,1024]{1,0:T(8,128)(2,1)}, bf16[256,1024]{1,0:T(8,128)(2,1)S(1)}, u32[]{:S(2)}) copy-start(bf16[256,1024]{1,0:T(8,128)(2,1)S(1)} %get-tuple-element.768) | copy-start | bytes 1572868
  369.9 6.3 collective-permute-start.3
  374.9 4.7 collective-permute-start.4
  379.7 40.2 %copy-start.13 = (bf16[1,256,1024]{2,1,0:T(8,128)(2,1)S(1)}, bf16[1,256,1024]{2,1,0:T(8,128)(2,1)}, u32[]{:S(2)}) copy-start(bf16[1,256,1024]{2,1,0:T(8,128)(2,1)} %param.29) | copy-start | bytes 1572868
  421.3 6.0 collective-permute-start.5
  424.8 4.7 collective-permute-start.6
  569.6 894.1 %reduce-scatter.3.cloned.1.call-start = ((), (), s32[]{:S(2)}) async-start(), calls=%async_computation.6 | async-start | bytes 12681216 | tf_op jit(solution)/shard_map/reduce_scatter | solution.py:250
  586.1 4.6 copy-start.2
  625.6 4.6 copy-start.2
  665.0 4.6 copy-start.2
  704.5 4.6 copy-start.2
  761.6 37.0 %collective-permute-start.7 = (bf16[1,256,2048]{1,2,0:T(8,128)(2,1)}, bf16[1,256,2048]{1,2,0:T(8,128)(2,1)}, u32[]{:S(2)}, u32[]{:S(2)}) collective-permute-start(bf16[1,256,2048]{1,2,0:T(8,128)(2,1)} %pad_maximum_fusion.4), channel_id=1, source_target_pairs={{1,0},{2,1},{3,2},{4,3},{5,4},{6,5},{7,6},{8,7},{9,8},{10,9},{11,1... | collective-permute-start | bytes 3145736 | tf_op jit(solution)/shard_map/ppermute | solution.py:14
  773.7 50.8 %collective-permute-start.8 = (bf16[1,256,2048]{1,0,2:T(2,128)(2,1)}, bf16[1,256,2048]{1,0,2:T(2,128)(2,1)S(1)}, u32[]{:S(2)}, u32[]{:S(2)}) collective-permute-start(bf16[1,256,2048]{1,0,2:T(2,128)(2,1)} %pad_maximum_fusion.1), channel_id=1, source_target_pairs={{2,0},{3,1},{4,2},{5,3},{6,4},{7,5},{8,6},{9,7},{10,8},{11,9},{12,... | collective-permute-start | bytes 3145736 | tf_op jit(solution)/shard_map/ppermute | solution.py:14
  788.9 47.9 %collective-permute-start.9 = (bf16[1,256,2048]{1,0,2:T(2,128)(2,1)S(1)}, bf16[1,256,2048]{1,0,2:T(2,128)(2,1)S(1)}, u32[]{:S(2)}, u32[]{:S(2)}) collective-permute-start(bf16[1,256,2048]{1,0,2:T(2,128)(2,1)S(1)} %pad_maximum_fusion.2), channel_id=1, source_target_pairs={{0,1},{1,2},{2,3},{3,4},{4,5},{5,6},{6,7},{7,8},{8,9},{9,10},{10,1... | collective-permute-start | bytes 3145736 | tf_op jit(solution)/shard_map/ppermute | solution.py:14
  836.8 19.4 %copy-start.5 = (f32[256,1024]{1,0:T(8,128)S(1)}, f32[256,1024]{1,0:T(8,128)}, u32[]{:S(2)}) copy-start(f32[256,1024]{1,0:T(8,128)} %copy-done.4) | copy-start | bytes 3145732
  836.8 19.4 %copy-start.15 = (bf16[4,1,256,4,64]{2,4,3,1,0:T(8,128)(2,1)S(1)}, bf16[4,1,256,4,64]{2,4,3,1,0:T(8,128)(2,1)}, u32[]{:S(2)}) copy-start(bf16[4,1,256,4,64]{2,4,3,1,0:T(8,128)(2,1)} %get-tuple-element.376) | copy-start | bytes 1572868
  836.8 19.4 %copy-start.18 = (f32[1024]{0:T(1024)S(1)}, f32[1024]{0:T(1024)}, u32[]{:S(2)}) copy-start(f32[1024]{0:T(1024)} %param.24) | copy-start | bytes 12292
  836.8 19.4 %copy-start.21 = (f32[256]{0:T(256)S(1)}, f32[256]{0:T(256)}, u32[]{:S(2)}) copy-start(f32[256]{0:T(256)} %copy-done.20) | copy-start | bytes 3076
  862.8 746.3 %all-reduce.2.cloned.1.call-start = ((), (), s32[]{:S(2)}) async-start(), calls=%async_computation.8 | async-start | bytes 262144 | tf_op jit(solution)/shard_map/psum | solution.py:177
  863.8 4.8 copy-start.9
  863.9 746.9 %copy-start.1 = (s32[16,1]{0,1:T(1,128)S(1)}, s32[16,1]{0,1:T(1,128)}, u32[]{:S(2)}) copy-start(s32[16,1]{0,1:T(1,128)} %param.28) | copy-start | bytes 196
  (13 other events, 24.0 us)
Sparse Core Ops, SparseCore 0:
  10.3 29.0 all-gather.3
  41.0 41.4 all-gather.5
  243.7 27.2 all-gather.7
  569.7 640.1 reduce-scatter.4
  1215.5 248.1 reduce-scatter.2
  1469.6 139.4 all-reduce.1
where the time goes:
time: 1640 us; the launch traced here: 1620 us
  waiting for transfers between devices  792 us (48%)
  local copies, waits for them, and re-layouts  350 us (21%)
  matrix products  175 us (11%)
  other arithmetic  172 us (10%)
  blocking collectives  71.5 us (4%)
  starting transfers between devices  34.8 us (2%)
    reduce_scatter x1, waiting for transfers between devices, on_device(): lax.psum_scatter(grad_wout, ('dp', 'ctx'), scatter_dimension=0, tiled=True)  340 us
    reduce_scatter x1, waiting for transfers between devices, on_device(): lax.psum_scatter(grad_wqkv, ('dp', 'ctx'), scatter_dimension=0, tiled=True)  235 us
    psum x1, waiting for transfers between devices, on_device(): grad_kernel = lax.psum(kernel_rows, ('dp', 'ctx'))  126 us
    gather x8, local copies, waits for them, and re-layouts, on_device(): jnp.take(table_whole[codebook], ids_whole[:, :, codebook], axis=0)  117 us
    ppermute x6, waiting for transfers between devices, from_behind(): lax.ppermute(value, axis, [(source, source + steps) for source in range(f...  75.4 us
    add x31, other arithmetic, back_step(): grad_input + taps * lax.dynamic_slice_in_dim(grad_padded, start_row, fram...  63.2 us
    dot_general x32, matrix products, block_scores(): jnp.einsum('rqhd,rkhd->rhqk', queries, key_block, preferred_element_type=...  52.4 us
    dynamic_update_slice x31, local copies, waits for them, and re-layouts, back_step(): lax.dynamic_update_index_in_dim(kernel_rows, row, tap_index, 0)  43.4 us
  transfers between devices with their start and end apart: 16, of which 11 were waited for; matrix products, arithmetic and copies ran while one was open for 31% of the time, Pallas kernels for 0%

commit v1 on v0

--- a/solution.py
+++ b/solution.py
@@ -174,7 +174,7 @@
             jnp.zeros((tap_count, model_width), jnp.float32),
         ),
     )
-    grad_kernel = lax.psum(kernel_rows, ("dp", "ctx"))
+    grad_kernel = jnp.sum(lax.all_gather(kernel_rows, ("dp", "ctx")), axis=0)
     grad_middle = (
         upstream.reshape(-1, model_width)
         + norm_back(middle_wide, conv_inverse, conv_gain, grad_input.reshape(-1, model_width))

time: 1640 us -> 1580 us (0.963)
  waiting for transfers between devices: 792 us -> 729 us
    psum x1 -> x0, waiting for transfers between devices: 126 us -> none  [on_device(): grad_kernel = lax.psum(kernel_rows, ('dp', 'ctx'))]
    all_gather x0 -> x1, waiting for transfers between devices: none -> 64.1 us  [on_device(): grad_kernel = jnp.sum(lax.all_gather(kernel_rows, ('dp', 'ctx')), axis=0)]
  transfers between devices with their start and end apart: 16 -> 16, of which waited for: 11 -> 11; matrix products, arithmetic and copies ran while one was open for 31% -> 32% of each run, Pallas kernels for 0% -> 0%
where the time goes in v1:
time: 1580 us; the launch traced here: 1560 us
  waiting for transfers between devices  729 us (46%)
  local copies, waits for them, and re-layouts  349 us (22%)
  other arithmetic  179 us (11%)
  matrix products  176 us (11%)
  blocking collectives  72.5 us (5%)
  starting transfers between devices  34.7 us (2%)
  between operations  15.9 us (1%)
    reduce_scatter x1, waiting for transfers between devices, on_device(): lax.psum_scatter(grad_wout, ('dp', 'ctx'), scatter_dimension=0, tiled=True)  336 us
    reduce_scatter x1, waiting for transfers between devices, on_device(): lax.psum_scatter(grad_wqkv, ('dp', 'ctx'), scatter_dimension=0, tiled=True)  238 us
    gather x8, local copies, waits for them, and re-layouts, on_device(): jnp.take(table_whole[codebook], ids_whole[:, :, codebook], axis=0)  117 us
    ppermute x6, waiting for transfers between devices, from_behind(): lax.ppermute(value, axis, [(source, source + steps) for source in range(f...  74.9 us
    all_gather x1, waiting for transfers between devices, on_device(): grad_kernel = jnp.sum(lax.all_gather(kernel_rows, ('dp', 'ctx')), axis=0)  64.1 us
    add x31, other arithmetic, back_step(): grad_input + taps * lax.dynamic_slice_in_dim(grad_padded, start_row, fram...  63.2 us
    dot_general x32, matrix products, block_scores(): jnp.einsum('rqhd,rkhd->rhqk', queries, key_block, preferred_element_type=...  52.9 us
    dynamic_update_slice x31, local copies, waits for them, and re-layouts, back_step(): lax.dynamic_update_index_in_dim(kernel_rows, row, tap_index, 0)  43.4 us
  transfers between devices with their start and end apart: 16, of which 11 were waited for; matrix products, arithmetic and copies ran while one was open for 32% of the time, Pallas kernels for 0%

profile of v1, /device:TPU:1, one launch (start us, length us, event | category | flops | bytes accessed | tf_op | source)
XLA Modules:
  0.0 1562.7 jit_solution(3428019035891964898)
XLA Ops:
  9.8 19.9 %all_gather.25 = s32[1,4096,8]{1,2,0:T(8,128)S(1)} all-gather(s32[1,256,8]{1,2,0:T(8,128)} %param.20), channel_id=1, replica_groups=mesh['dp'=8,'ctx'=16] {'ctx'}, dimensions={1}, use_global_device_ids=true | all-gather | bytes 139264 | tf_op jit(solution)/shard_map/all_gather | solution.py:74
  30.4 8.9 all-gather.7.cloned.1.call-done
  41.0 12.1 gather_fusion.2
  53.1 14.9 gather_fusion.3
  68.0 14.9 gather_fusion.4
  82.9 14.9 gather_fusion.5
  97.8 14.9 gather_fusion.6
  112.7 15.0 gather_fusion.7
  127.8 14.9 gather_fusion
  142.7 14.9 gather_fusion.1
  157.6 8.9 add_convert_fusion
  166.5 16.7 %copy.311 = bf16[1,4096,64]{2,0,1:T(2,128)(2,1)S(1)} copy(bf16[1,4096,64]{2,1,0:T(8,128)(2,1)S(1)} %add_convert_fusion) | data formatting | bytes 1048576 | tf_op jit(solution)/shard_map/convert_element_type | solution.py:82
  183.8 22.4 %reduce.52 = bf16[4096,64]{1,0:T(8,128)(2,1)S(1)} reduce(bf16[4096,1,64]{2,1,0:T(2,128)(2,1)S(1)} %bitcast.412, bf16[]{:T(256)} %broadcast.243), dimensions={1}, to_apply=%bitcast.324.reduce_sub_computation | reduce | bytes 1048578
  206.9 17.4 %all_to_all.4 = bf16[16,2,8192]{2,1,0:T(2,128)(2,1)S(1)} all-to-all(bf16[16,2,8192]{2,1,0:T(2,128)(2,1)S(1)} %reshape.828), channel_id=1, replica_groups=mesh['dp'=8,'ctx'=16] {'ctx'}, dimensions={0} | all-to-all | bytes 1048576 | tf_op jit(solution)/shard_map/all_to_all | solution.py:81
  247.8 11.2 collective-permute-done
  259.0 22.5 %collective-permute-done.1 = bf16[1,256,2048]{2,1,0:T(8,128)(2,1)} collective-permute-done((bf16[1,256,2048]{2,1,0:T(8,128)(2,1)S(1)}, bf16[1,256,2048]{2,1,0:T(8,128)(2,1)}, u32[]{:S(2)}, u32[]{:S(2)}) %collective-permute-start.1) | collective-permute-done | bytes 1048608 | tf_op jit(solution)/shard_map/ppermute | solution.py:14
  301.0 66.2 %while.56 = (s32[]{:T(128)}, bf16[4,1,256,4,64]{2,4,3,1,0:T(8,128)(2,1)}, s32[4]{0:T(128)S(1)}, bf16[1,4,256,16,64]{2,1,4,3,0:T(4,128)(2,1)}, bf16[1,256,16,64]{...) while((s32[]{:T(128)}, ...), condition=%wide.region_10.12_spmd, body=%wide.region_4.11_spmd.sunk | while | flops 282916864 | bytes 20639508 | solution.py:129
  380.1 40.1 %while.58 = (s32[]{:T(128)}, f32[1,256,1024]{2,1,0:T(8,128)S(1)}, f32[31,1024]{1,0:T(8,128)}, f32[1,286,1024]{2,1,0:T(8,128)S(1)}, s32[]{:T(128)}, /*index=5*/s32[]{:T(128)}) while((s32[]{:T(128)}, f32[1,256,1024]{2,1,0:T(8,128)S(1)}, f32[31,1024]{1,0:T(8,128)}, f32[1,286,1024]{2,1,0:T(8,128)S(1)}, s32[]{:T(128)}, ...), condition=%wide.region_13.15_spmd.clone, body=%wide.region_12.14_spmd.clone.sunk | while | flops 786435 | bytes 3158103 | solution.py:146
  432.0 130.4 %while.59 = (s32[]{:T(128)}, f32[1,256,1024]{2,1,0:T(8,128)S(1)}, f32[31,1024]{1,0:T(8,128)}, f32[31,1024]{1,0:T(8,128)}, f32[1,286,1024]{2,1,0:T(8,128)}, /*ind...) while((s32[]{:T(128)}, f32[1,256,1024]{2,1,0:T(8,128)S(1)}, ...), condition=%wide.region_16.18_spmd.clone, body=%wide.region_14.17_spmd.clone.sunk | while | flops 1309703 | bytes 5267637 | solution.py:168
  569.9 8.7 reduce-scatter.3.cloned.1.call-start
  578.6 159.0 %while.57 = (s32[]{:T(128)}, bf16[4,1,256,4,64]{2,4,3,1,0:T(8,128)(2,1)}, f32[4,1,1024,4,64]{2,4,3,1,0:T(8,128)}, f32[4,1,1024,4,64]{2,4,3,1,0:T(8,128)}, s32[4]...) while((s32[]{:T(128)}, ...), condition=%wide.region_25.27_spmd, body=%wide.region_18.26_spmd.sunk | while | flops 716965888 | bytes 64713528 | solution.py:218
  638.9 7.5 fusion.199
  767.1 8.1 pad_maximum_fusion.1
  801.4 24.8 %collective-permute-done.8 = bf16[1,256,2048]{1,0,2:T(2,128)(2,1)S(1)} collective-permute-done((bf16[1,256,2048]{1,0,2:T(2,128)(2,1)}, bf16[1,256,2048]{1,0,2:T(2,128)(2,1)S(1)}, u32[]{:S(2)}, u32[]{:S(2)}) %collective-permute-start.8) | collective-permute-done | bytes 1048608 | tf_op jit(solution)/shard_map/ppermute | solution.py:14
  826.2 11.5 collective-permute-done.9
  837.7 19.2 %fusion.105 = bf16[1,256,2048]{1,0,2:T(2,128)(2,1)S(1)} fusion(bf16[1,256,2048]{1,0,2:T(2,128)(2,1)S(1)} %collective-permute-done.9, bf16[1,256,2048]{1,0,2:T(2,128)(2,1)S(1)} %collective-permute-done.8, f32[1,256,2048]{1,2,0:T(8,128)S(1)} %convert_element_type.227, f32[1,256,1024]{1,0,2:T(1,128)S(1)} %get-tuple-element.771, ...), kind=kLoop, calls=%fused_computation.122 | loop fusion | flops 3670016 | bytes 7340032 | tf_op jit(solution)/shard_map/convert_element_type | solution.py:236
  870.8 336.3 %reduce-scatter.5.cloned.1.call-done = f32[8,1024]{1,0:T(8,128)} async-done(((f32[1024,1024]{1,0:T(8,128)}), f32[8,1024]{1,0:T(8,128)}) %reduce-scatter.5.cloned.1.call-update) | async-done | bytes 32784 | tf_op jit(solution)/shard_map/reduce_scatter | solution.py:251
  1207.9 17.4 %all_gather.29 = bf16[128,1024]{1,0:T(8,128)(2,1)S(1)} all-gather(bf16[8,1024]{1,0:T(8,128)(2,1)S(1)} %convert_element_type.235), channel_id=1, replica_groups=mesh['dp'=8,'ctx'=16] {'ctx'}, dimensions={0}, use_global_device_ids=true | all-gather | bytes 278528 | tf_op jit(solution)/shard_map/all_gather | solution.py:257
  1226.1 237.7 %reduce-scatter.3.cloned.1.call-done = f32[8,3072]{1,0:T(8,128)} async-done(((f32[1024,3072]{1,0:T(8,128)}), f32[8,3072]{1,0:T(8,128)}) %reduce-scatter.3.cloned.1.call-update) | async-done | bytes 98320 | tf_op jit(solution)/shard_map/reduce_scatter | solution.py:250
  1464.7 17.8 %all_gather.28 = bf16[128,3072]{1,0:T(8,128)(2,1)S(1)} all-gather(bf16[8,3072]{1,0:T(8,128)(2,1)S(1)} %convert_element_type.233), channel_id=1, replica_groups=mesh['dp'=8,'ctx'=16] {'ctx'}, dimensions={0}, use_global_device_ids=true | all-gather | bytes 835584 | tf_op jit(solution)/shard_map/all_gather | solution.py:254
  1483.8 64.1 %all-gather.13.cloned.1.call-done = f32[128,31,1024]{2,1,0:T(8,128)} async-done(((f32[1,31,1024]{2,1,0:T(8,128)}), f32[128,31,1024]{2,1,0:T(8,128)}) %all-gather.13.cloned.1.call-update) | async-done | bytes 16252944 | tf_op jit(solution)/shard_map/all_gather | solution.py:177
  1547.9 7.5 reduce_sum.101
  (430 shorter events, 535.3 us)
Async XLA Ops:
  7.2 236.5 %copy-start = (s32[16,1]{0,1:T(1,128)S(1)}, s32[16,1]{0,1:T(1,128)}, u32[]{:S(2)}) copy-start(s32[16,1]{0,1:T(1,128)} %param.28) | copy-start | bytes 196
  7.2 32.2 %all-gather.7.cloned.1.call-start = ((), (), s32[]{:S(2)}) async-start(), calls=%async_computation.3 | async-start | bytes 2359296 | tf_op jit(solution)/shard_map/all_gather | solution.py:75
  9.0 220.5 %all-gather.9.cloned.1.call-start = ((), (), s32[]{:S(2)}) async-start(), calls=%async_computation.4 | async-start | bytes 7077888 | tf_op jit(solution)/shard_map/all_gather | solution.py:85
  9.8 357.4 %all-gather.11.cloned.1.call-start = ((), (), s32[]{:S(2)}) async-start(), calls=%async_computation.5 | async-start | bytes 2359296 | tf_op jit(solution)/shard_map/all_gather | solution.py:86
  142.7 14.9 copy-start.10
  229.2 5.6 copy-start.4
  229.5 15.5 copy-start.22
  236.0 23.0 %collective-permute-start = (bf16[1,256,2048]{2,1,0:T(8,128)(2,1)S(1)}, bf16[1,256,2048]{2,1,0:T(8,128)(2,1)}, u32[]{:S(2)}, u32[]{:S(2)}) collective-permute-start(bf16[1,256,2048]{2,1,0:T(8,128)(2,1)S(1)} %get-tuple-element.746), channel_id=1, source_target_pairs={{0,1},{1,2},{2,3},{3,4},{4,5},{5,6},{6,7},{7,8},{8,9},{9,10},{10,1... | collective-permute-start | bytes 3145736 | tf_op jit(solution)/shard_map/ppermute | solution.py:14
  239.2 42.2 %collective-permute-start.1 = (bf16[1,256,2048]{2,1,0:T(8,128)(2,1)S(1)}, bf16[1,256,2048]{2,1,0:T(8,128)(2,1)}, u32[]{:S(2)}, u32[]{:S(2)}) collective-permute-start(bf16[1,256,2048]{2,1,0:T(8,128)(2,1)S(1)} %get-tuple-element.746), channel_id=1, source_target_pairs={{0,2},{1,3},{2,4},{3,5},{4,6},{5,7},{6,8},{7,9},{8,10},{9,11},{10,... | collective-permute-start | bytes 3145736 | tf_op jit(solution)/shard_map/ppermute | solution.py:14
  242.3 44.1 %collective-permute-start.2 = (bf16[1,256,2048]{2,1,0:T(8,128)(2,1)S(1)}, bf16[1,256,2048]{2,1,0:T(8,128)(2,1)}, u32[]{:S(2)}, u32[]{:S(2)}) collective-permute-start(bf16[1,256,2048]{2,1,0:T(8,128)(2,1)S(1)} %get-tuple-element.746), channel_id=1, source_target_pairs={{1,0},{2,1},{3,2},{4,3},{5,4},{6,5},{7,6},{8,7},{9,8},{10,9},{11,1... | collective-permute-start | bytes 3145736 | tf_op jit(solution)/shard_map/ppermute | solution.py:14
  243.6 963.5 %reduce-scatter.5.cloned.1.call-start = ((), (), s32[]{:S(2)}) async-start(), calls=%async_computation.7 | async-start | bytes 4227072 | tf_op jit(solution)/shard_map/reduce_scatter | solution.py:251
  370.0 50.2 %copy-start.6 = (bf16[256,1024]{1,0:T(8,128)(2,1)}, bf16[256,1024]{1,0:T(8,128)(2,1)S(1)}, u32[]{:S(2)}) copy-start(bf16[256,1024]{1,0:T(8,128)(2,1)S(1)} %get-tuple-element.768) | copy-start | bytes 1572868
  370.3 6.3 collective-permute-start.3
  375.2 4.7 collective-permute-start.4
  380.1 40.2 %copy-start.13 = (bf16[1,256,1024]{2,1,0:T(8,128)(2,1)S(1)}, bf16[1,256,1024]{2,1,0:T(8,128)(2,1)}, u32[]{:S(2)}) copy-start(bf16[1,256,1024]{2,1,0:T(8,128)(2,1)} %param.29) | copy-start | bytes 1572868
  421.7 6.0 collective-permute-start.5
  425.1 4.7 collective-permute-start.6
  569.9 893.9 %reduce-scatter.3.cloned.1.call-start = ((), (), s32[]{:S(2)}) async-start(), calls=%async_computation.6 | async-start | bytes 12681216 | tf_op jit(solution)/shard_map/reduce_scatter | solution.py:250
  586.5 4.6 copy-start.2
  626.2 4.6 copy-start.2
  666.0 4.6 copy-start.2
  705.7 4.6 copy-start.2
  763.0 37.0 %collective-permute-start.7 = (bf16[1,256,2048]{1,2,0:T(8,128)(2,1)}, bf16[1,256,2048]{1,2,0:T(8,128)(2,1)}, u32[]{:S(2)}, u32[]{:S(2)}) collective-permute-start(bf16[1,256,2048]{1,2,0:T(8,128)(2,1)} %pad_maximum_fusion.4), channel_id=1, source_target_pairs={{1,0},{2,1},{3,2},{4,3},{5,4},{6,5},{7,6},{8,7},{9,8},{10,9},{11,1... | collective-permute-start | bytes 3145736 | tf_op jit(solution)/shard_map/ppermute | solution.py:14
  775.2 51.1 %collective-permute-start.8 = (bf16[1,256,2048]{1,0,2:T(2,128)(2,1)}, bf16[1,256,2048]{1,0,2:T(2,128)(2,1)S(1)}, u32[]{:S(2)}, u32[]{:S(2)}) collective-permute-start(bf16[1,256,2048]{1,0,2:T(2,128)(2,1)} %pad_maximum_fusion.1), channel_id=1, source_target_pairs={{2,0},{3,1},{4,2},{5,3},{6,4},{7,5},{8,6},{9,7},{10,8},{11,9},{12,... | collective-permute-start | bytes 3145736 | tf_op jit(solution)/shard_map/ppermute | solution.py:14
  790.3 47.4 %collective-permute-start.9 = (bf16[1,256,2048]{1,0,2:T(2,128)(2,1)S(1)}, bf16[1,256,2048]{1,0,2:T(2,128)(2,1)S(1)}, u32[]{:S(2)}, u32[]{:S(2)}) collective-permute-start(bf16[1,256,2048]{1,0,2:T(2,128)(2,1)S(1)} %pad_maximum_fusion.2), channel_id=1, source_target_pairs={{0,1},{1,2},{2,3},{3,4},{4,5},{5,6},{6,7},{7,8},{8,9},{9,10},{10,1... | collective-permute-start | bytes 3145736 | tf_op jit(solution)/shard_map/ppermute | solution.py:14
  837.7 19.4 %copy-start.5 = (f32[256,1024]{1,0:T(8,128)S(1)}, f32[256,1024]{1,0:T(8,128)}, u32[]{:S(2)}) copy-start(f32[256,1024]{1,0:T(8,128)} %copy-done.4) | copy-start | bytes 3145732
  837.7 19.4 %copy-start.15 = (bf16[4,1,256,4,64]{2,4,3,1,0:T(8,128)(2,1)S(1)}, bf16[4,1,256,4,64]{2,4,3,1,0:T(8,128)(2,1)}, u32[]{:S(2)}) copy-start(bf16[4,1,256,4,64]{2,4,3,1,0:T(8,128)(2,1)} %get-tuple-element.376) | copy-start | bytes 1572868
  837.7 19.4 %copy-start.18 = (f32[1024]{0:T(1024)S(1)}, f32[1024]{0:T(1024)}, u32[]{:S(2)}) copy-start(f32[1024]{0:T(1024)} %param.24) | copy-start | bytes 12292
  837.7 19.4 %copy-start.21 = (f32[256]{0:T(256)S(1)}, f32[256]{0:T(256)}, u32[]{:S(2)}) copy-start(f32[256]{0:T(256)} %copy-done.20) | copy-start | bytes 3076
  863.7 684.1 %all-gather.13.cloned.1.call-start = ((), (), s32[]{:S(2)}) async-start(), calls=%async_computation.8 | async-start | bytes 16908288 | tf_op jit(solution)/shard_map/all_gather | solution.py:177
  864.8 4.8 copy-start.9
  1547.9 7.5 copy-start.1
  (13 other events, 23.8 us)
Sparse Core Ops, SparseCore 0:
  10.3 29.0 all-gather.6
  41.0 41.4 all-gather.8
  243.7 27.2 all-gather.10
  570.0 637.0 reduce-scatter.4
  1212.7 251.0 reduce-scatter.2
  1467.8 80.0 all-gather.12
